TPU v7x, 32 devices: a whole 2x2x4 slice. The times are simulated.
32 devices in a mesh: snp: 8 (over z, y), samp: 4 (over x, core).
Axes of the slice: x: 2, y: 2, z: 4, core: 2. Of those that a mesh axis runs over, the one named last changes fastest.
Arguments:
- genotypes: bfloat16 [1536, 5120], P('samp', 'snp'), may hold values from -0.076171875 to 0.076171875
- responses: float32 [3072, 1536], P('snp', 'samp'), may hold values from -6 to 6
- weights: float32 [1024, 64, 128], P('snp'), may hold values from -6 to 6
- pattern: int32 [1024, 2], P('snp'), may hold values from 0 to 45, as said below
- entry_count: int32 [8], P('snp'), may hold values from 64 to 128, as said below
- tile_slot: int32 [46], replicated, may hold values from 0 to 47, as said below
- penalty: float32 [46], replicated, may hold values from 0.5 to 5
Outputs:
- new_weights: float32 [1024, 64, 128], P('snp')
Inputs may be any that keep to these rules, and one draw needn't show every extreme that they name: `pattern`: column 0 is a block below 5, column 1 a tile below 46; within one segment's 128 rows no (block, tile) pair repeats. `entry_count`: some segment has all 128 entries live. `tile_slot`: distinct slots.
All inputs are finite; a program needn't handle non-finite values.
Results may differ from a plain program's by a relative error of at most 0.0032.
Values may be sent and summed in bfloat16 or wider, within the bound.
No kernel may reach another device: no remote copies, remote signals or barrier semaphores. Data moves between devices by JAX's collectives and lax.ppermute only.
A program may use at most 128 MiB of HBM per device.

v0:
```python
import jax
import jax.numpy as jnp
from jax import lax
from jax.sharding import PartitionSpec as P

ITERS = 2
step_scale = 0.3


def shrink_soft(current, gradient, cutoff, active):
    shifted = current + step_scale * gradient
    shrunk = jnp.sign(shifted) * jnp.maximum(jnp.abs(shifted) - cutoff, jnp.float32(0.0))
    return jnp.where(active[:, None, None], shrunk, jnp.float32(0.0))


def per_device(genotypes, responses, weights, pattern, entry_count, tile_slot, penalty):
    sample_count = genotypes.shape[0]
    entries, tile_width, block_width = weights.shape
    block_count = genotypes.shape[1] // block_width
    own_rows = responses.shape[0]
    owners = lax.axis_size("snp")
    own_slots = own_rows // tile_width
    slot_total = owners * own_slots
    cells = slot_total * block_count
    geno_blocks = genotypes.reshape(sample_count, block_count, block_width)
    blk = pattern[:, 0]
    tile = pattern[:, 1]
    tile_hot = tile[:, None] == jnp.arange(penalty.shape[0], dtype=jnp.int32)[None, :]
    slot_ids = jnp.sum(jnp.where(tile_hot, tile_slot[None, :], 0), axis=1)
    per_entry = jnp.sum(jnp.where(tile_hot, penalty[None, :], jnp.float32(0.0)), axis=1)
    cutoff = step_scale * per_entry[:, None, None]
    cell = slot_ids * block_count + blk
    cell_hot = (cell[:, None] == jnp.arange(cells, dtype=jnp.int32)[None, :]).astype(jnp.bfloat16)
    active = jnp.arange(entries, dtype=jnp.int32) < entry_count[0]
    current = jnp.where(active[:, None, None], weights, jnp.float32(0.0))
    for sweep in range(ITERS):
        weight_bf = current.astype(jnp.bfloat16)
        dense = jnp.einsum(
            "ec,epk->cpk", cell_hot, weight_bf, preferred_element_type=jnp.float32
        ).astype(jnp.bfloat16)
        dense = dense.reshape(slot_total, block_count, tile_width, block_width)
        partial = jnp.einsum(
            "jbpk,sbk->jps", dense, geno_blocks, preferred_element_type=jnp.float32
        ).astype(jnp.bfloat16)
        partial = partial.reshape(owners, own_rows, sample_count)
        gathered = lax.all_to_all(partial, "snp", 0, 0, tiled=False)
        prediction = jnp.sum(gathered.astype(jnp.float32), axis=0)
        residual = (responses - prediction).astype(jnp.bfloat16)
        shard_rows = lax.all_gather(residual, "snp", axis=0, tiled=True)
        blocks = shard_rows.reshape(slot_total, tile_width, sample_count)
        full = jnp.einsum(
            "jps,sbk->jbpk", blocks, geno_blocks, preferred_element_type=jnp.float32
        ).reshape(cells, tile_width, block_width)
        local_gradient = jnp.take(full, cell, axis=0, mode="clip")
        if SPLIT_SAMP:
            part = lax.psum_scatter(local_gradient, "sc", scatter_dimension=0, tiled=True)
            part = lax.psum(part, "sx")
            gradient = lax.all_gather(part, "sc", axis=0, tiled=True)
        else:
            gradient = lax.psum(local_gradient, "samp")
        current = shrink_soft(current, gradient, cutoff, active)
    return current


SPLIT_SAMP = True


def solution(mesh):
    snp_size, samp_size = mesh.devices.shape
    samp = "samp"
    if SPLIT_SAMP:
        devices = mesh.devices.reshape(snp_size, 2, samp_size // 2)
        mesh = jax.sharding.Mesh(devices, ("snp", "sx", "sc"))
        samp = ("sx", "sc")
    in_specs = (
        P(samp, "snp"),
        P("snp", samp),
        P("snp", None, None),
        P("snp", None),
        P("snp"),
        P(),
        P(),
    )
    out_specs = P("snp", None, None)
    return jax.shard_map(
        per_device, mesh=mesh, in_specs=in_specs, out_specs=out_specs, check_vma=False
    )
```

profile of v0, /device:TPU:0, one launch (start us, length us, event | category | flops | bytes accessed | tf_op | source)
XLA Modules:
  0.0 482.6 jit_solution(14898244865369778887)
XLA Ops:
  6.5 0.0 all-gather.5.cloned.1.call-start
  7.2 0.7 slice_bitcast_fusion
  7.9 0.7 select_reduce_fusion.1
  8.6 0.7 fusion.7
  9.3 1.3 copy.36
  10.6 2.6 select_convert_fusion
  13.2 2.0 convolution_convert_fusion.1
  15.3 1.0 copy.35
  16.3 2.6 bitcast_convert_fusion.1
  18.9 0.0 copy-start
  18.9 61.1 %all_to_all.10 = bf16[8,384,384]{2,1,0:T(8,128)(2,1)S(1)} all-to-all(bf16[8,384,384]{2,1,0:T(8,128)(2,1)S(1)} %bitcast.62), channel_id=1, replica_groups=mesh['snp'=8,'sx'=2,'sc'=2] {'snp'}, dimensions={0} | all-to-all | bytes 4718592 | tf_op jit(solution)/shard_map/all_to_all | solution.py:46
  80.0 0.3 convert_reduce_fusion.1
  80.3 0.0 copy-done
  80.4 0.8 subtract_convert_fusion.1
  81.2 0.0 all-gather.5.cloned.1.call-update
  81.2 0.0 reduce-scatter.3.cloned.1.call-start
  81.2 51.2 %all-gather.5.cloned.1.call-done = bf16[3072,384]{1,0:T(8,128)(2,1)} async-done(((bf16[384,384]{1,0:T(8,128)(2,1)}), bf16[3072,384]{1,0:T(8,128)(2,1)}) %all-gather.5.cloned.1.call-update) | async-done | bytes 2359312 | tf_op jit(solution)/shard_map/all_gather | solution.py:49
  132.4 7.2 %fusion.9 = f32[48,64,5,128]{3,1,2,0:T(8,128)} fusion(bf16[48,64,384,1]{2,1,3,0:T(8,128)(2,1)} %bitcast.64, bf16[384,5,128,1]{0,2,1,3:T(8,128)(2,1)S(1)} %bitcast.57), kind=kOutput, calls=%fused_computation.29 | convolution fusion | flops 1509949440 | bytes 10715136 | tf_op jit(solution)/shard_map/jps,sbk->jbpk/dot_general | solution.py:51
  139.6 6.1 %gather_fusion = f32[128,64,128]{2,1,0:T(8,128)} fusion(f32[240,64,128]{2,1,0:T(8,128)} %bitcast.55, s32[1024]{0:T(1024)S(1)} %pad_clamp_fusion), kind=kCustom, calls=%fused_computation | custom fusion | bytes 8389120 | tf_op jit(solution)/shard_map/jit(_take)/gather | solution.py:54
  145.6 0.0 copy-start.1
  145.7 0.0 reduce-scatter.3.cloned.1.call-update
  145.7 0.0 all-reduce.3.cloned.1.call-start
  145.7 10.7 %reduce-scatter.3.cloned.1.call-done = f32[64,64,128]{2,1,0:T(8,128)} async-done(((f32[128,64,128]{2,1,0:T(8,128)}), f32[64,64,128]{2,1,0:T(8,128)}) %reduce-scatter.3.cloned.1.call-update) | async-done | bytes 2097168 | tf_op jit(solution)/shard_map/reduce_scatter | solution.py:56
  156.4 0.0 all-reduce.3.cloned.1.call-update
  156.4 0.0 all-gather.7.cloned.1.call-start
  156.5 66.6 %all-reduce.3.cloned.1.call-done = f32[64,64,128]{2,1,0:T(8,128)} async-done(((f32[64,64,128]{2,1,0:T(8,128)}), f32[64,64,128]{2,1,0:T(8,128)}) %all-reduce.3.cloned.1.call-update) | async-done | bytes 2097168 | tf_op jit(solution)/shard_map/psum | solution.py:57
  223.0 0.0 all-gather.7.cloned.1.call-update
  223.1 0.2 all-gather.9.cloned.1.call-start
  223.3 0.0 copy-done.1
  223.3 0.1 select_reduce_fusion
  223.4 14.7 %all-gather.7.cloned.1.call-done = f32[128,64,128]{2,1,0:T(8,128)} async-done(((f32[64,64,128]{2,1,0:T(8,128)}), f32[128,64,128]{2,1,0:T(8,128)}) %all-gather.7.cloned.1.call-update) | async-done | bytes 4194320 | tf_op jit(solution)/shard_map/all_gather | solution.py:58
  238.1 4.7 fusion.8
  242.9 2.0 convolution_convert_fusion
  244.9 1.0 copy.40
  245.9 2.6 bitcast_convert_fusion
  248.6 59.8 %all_to_all.11 = bf16[8,384,384]{2,1,0:T(8,128)(2,1)S(1)} all-to-all(bf16[8,384,384]{2,1,0:T(8,128)(2,1)S(1)} %bitcast.63), channel_id=1, replica_groups=mesh['snp'=8,'sx'=2,'sc'=2] {'snp'}, dimensions={0} | all-to-all | bytes 4718592 | tf_op jit(solution)/shard_map/all_to_all | solution.py:46
  308.4 0.3 convert_reduce_fusion
  308.7 0.8 subtract_convert_fusion
  309.5 0.0 all-gather.9.cloned.1.call-update
  309.6 0.0 reduce-scatter.5.cloned.1.call-start
  309.6 51.2 %all-gather.9.cloned.1.call-done = bf16[3072,384]{1,0:T(8,128)(2,1)} async-done(((bf16[384,384]{1,0:T(8,128)(2,1)}), bf16[3072,384]{1,0:T(8,128)(2,1)}) %all-gather.9.cloned.1.call-update) | async-done | bytes 2359312 | tf_op jit(solution)/shard_map/all_gather | solution.py:49
  360.8 7.2 %fusion.10 = f32[48,64,5,128]{3,1,2,0:T(8,128)} fusion(bf16[48,64,384,1]{2,1,3,0:T(8,128)(2,1)} %bitcast.65, bf16[384,5,128,1]{0,2,1,3:T(8,128)(2,1)S(1)} %bitcast.59), kind=kOutput, calls=%fused_computation.30 | convolution fusion | flops 1509949440 | bytes 10715136 | tf_op jit(solution)/shard_map/jps,sbk->jbpk/dot_general | solution.py:51
  368.0 6.1 %gather_fusion.1 = f32[128,64,128]{2,1,0:T(8,128)} fusion(f32[240,64,128]{2,1,0:T(8,128)} %bitcast.54, s32[1024]{0:T(1024)S(1)} %pad_clamp_fusion), kind=kCustom, calls=%fused_computation.1 | custom fusion | bytes 8389120 | tf_op jit(solution)/shard_map/jit(_take)/gather | solution.py:54
  374.1 0.0 reduce-scatter.5.cloned.1.call-update
  374.1 0.0 all-reduce.5.cloned.1.call-start
  374.1 10.7 %reduce-scatter.5.cloned.1.call-done = f32[64,64,128]{2,1,0:T(8,128)} async-done(((f32[128,64,128]{2,1,0:T(8,128)}), f32[64,64,128]{2,1,0:T(8,128)}) %reduce-scatter.5.cloned.1.call-update) | async-done | bytes 2097168 | tf_op jit(solution)/shard_map/reduce_scatter | solution.py:56
  384.8 0.0 all-reduce.5.cloned.1.call-update
  384.9 0.0 all-gather.11.cloned.1.call-start
  384.9 66.5 %all-reduce.5.cloned.1.call-done = f32[64,64,128]{2,1,0:T(8,128)} async-done(((f32[64,64,128]{2,1,0:T(8,128)}), f32[64,64,128]{2,1,0:T(8,128)}) %all-reduce.5.cloned.1.call-update) | async-done | bytes 2097168 | tf_op jit(solution)/shard_map/psum | solution.py:57
  451.4 0.0 all-gather.11.cloned.1.call-update
  451.5 15.2 %all-gather.11.cloned.1.call-done = f32[128,64,128]{2,1,0:T(8,128)} async-done(((f32[64,64,128]{2,1,0:T(8,128)}), f32[128,64,128]{2,1,0:T(8,128)}) %all-gather.11.cloned.1.call-update) | async-done | bytes 4194320 | tf_op jit(solution)/shard_map/all_gather | solution.py:58
  466.7 9.1 %multiply_select_fusion = f32[128,64,128]{2,1,0:T(8,128)} fusion(f32[128,64,128]{2,1,0:T(8,128)} %all-gather.11.cloned.1.call-done, f32[128]{0:T(128)S(1)} %broadcast_multiply_fusion, pred[128]{0:T(512)(128)(4,1)S(1)} %iota_compare_fusion.2, f32[128,64,128]{2,1,0:T(8,128)} %all-gather.7.cloned.1.call-done, f32[128,64,128]{2,1,0:T(8,128)} %param.9), kind=kLoop, calls=%fused_computation.6 | loop fusion | flops 17825792 | bytes 16777856 | tf_op jit(solution)/shard_map/jit(_where)/select_n | solution.py:13
  (3 shorter events, 0.0 us)
Async XLA Ops:
  6.5 125.9 %all-gather.5.cloned.1.call-start = ((), (), s32[]{:S(2)}) async-start(), calls=%async_computation.4 | async-start | bytes 2654208 | tf_op jit(solution)/shard_map/all_gather | solution.py:49
  18.9 61.4 %copy-start = (f32[384,384]{1,0:T(8,128)S(1)}, f32[384,384]{1,0:T(8,128)}, u32[]{:S(2)}) copy-start(f32[384,384]{1,0:T(8,128)} %param.8) | copy-start | bytes 1769476
  81.2 75.2 %reduce-scatter.3.cloned.1.call-start = ((), (), s32[]{:S(2)}) async-start(), calls=%async_computation.5 | async-start | bytes 6291456 | tf_op jit(solution)/shard_map/reduce_scatter | solution.py:56
  145.6 77.6 %copy-start.1 = (f32[46]{0:T(128)S(1)}, f32[46]{0:T(128)}, u32[]{:S(2)}) copy-start(f32[46]{0:T(128)} %param.13) | copy-start | bytes 556
  145.7 77.4 %all-reduce.3.cloned.1.call-start = ((), (), s32[]{:S(2)}) async-start(), calls=%async_computation.6 | async-start | bytes 4194304 | tf_op jit(solution)/shard_map/psum | solution.py:57
  156.4 81.7 %all-gather.7.cloned.1.call-start = ((), (), s32[]{:S(2)}) async-start(), calls=%async_computation.7 | async-start | bytes 6291456 | tf_op jit(solution)/shard_map/all_gather | solution.py:58
  223.1 137.8 %all-gather.9.cloned.1.call-start = ((), (), s32[]{:S(2)}) async-start(), calls=%async_computation.8 | async-start | bytes 2654208 | tf_op jit(solution)/shard_map/all_gather | solution.py:49
  309.6 75.3 %reduce-scatter.5.cloned.1.call-start = ((), (), s32[]{:S(2)}) async-start(), calls=%async_computation.9 | async-start | bytes 6291456 | tf_op jit(solution)/shard_map/reduce_scatter | solution.py:56
  374.1 77.3 %all-reduce.5.cloned.1.call-start = ((), (), s32[]{:S(2)}) async-start(), calls=%async_computation.10 | async-start | bytes 4194304 | tf_op jit(solution)/shard_map/psum | solution.py:57
  384.9 81.8 %all-gather.11.cloned.1.call-start = ((), (), s32[]{:S(2)}) async-start(), calls=%async_computation.11 | async-start | bytes 6291456 | tf_op jit(solution)/shard_map/all_gather | solution.py:58
Sparse Core Ops, SparseCore 0:
  81.3 51.0 all-gather.4
  145.8 10.5 reduce-scatter.2
  158.8 64.1 all-reduce.2
  224.4 13.6 all-gather.6
  309.7 51.1 all-gather.8
  374.2 10.5 reduce-scatter.4
  387.2 64.1 all-reduce.4
  453.0 13.6 all-gather.10
where the time goes:
time: 483 us
  waiting for transfers between devices  287 us (59%)
  blocking collectives  121 us (25%)
  matrix products  23.6 us (5%)
  other arithmetic  20.2 us (4%)
  local copies, waits for them, and re-layouts  16.1 us (3%)
  between operations  14.3 us (3%)
    psum x2, waiting for transfers between devices, per_device(): part = lax.psum(part, 'sx')  133 us
    all_to_all x2, blocking collectives, per_device(): gathered = lax.all_to_all(partial, 'snp', 0, 0, tiled=False)  121 us
    all_gather x2, waiting for transfers between devices, per_device(): shard_rows = lax.all_gather(residual, 'snp', axis=0, tiled=True)  102 us
    all_gather x2, waiting for transfers between devices, per_device(): gradient = lax.all_gather(part, 'sc', axis=0, tiled=True)  30 us
    reduce_scatter x2, waiting for transfers between devices, per_device(): lax.psum_scatter(local_gradient, 'sc', scatter_dimension=0, tiled=True)  21.4 us
    dot_general x2, matrix products, per_device(): jnp.einsum('jps,sbk->jbpk', blocks, geno_blocks, preferred_element_type=j...  14.3 us
    gather x2, local copies, waits for them, and re-layouts, per_device(): local_gradient = jnp.take(full, cell, axis=0, mode='clip')  12.1 us
  transfers between devices with their start and end apart: 8, of which 8 were waited for; matrix products, arithmetic and copies ran while one was open for 0% of the time, Pallas kernels for 0%

commit v1 on v0

--- a/solution.py
+++ b/solution.py
@@ -5,6 +5,16 @@
 
 ITERS = 2
 step_scale = 0.3
+
+
+def gather_by_hops(x, axis, dim):
+    n_dev = lax.axis_size(axis)
+    current, shards = (x, [x])
+    for _ in range(n_dev - 1):
+        current = lax.ppermute(current, axis, [(i, (i + 1) % n_dev) for i in range(n_dev)])
+        shards.insert(0, current)
+    row_of_blocks = jnp.concatenate(shards, axis=dim)
+    return jnp.roll(row_of_blocks, (lax.axis_index(axis) + 1) * x.shape[dim], axis=dim)
 
 
 def shrink_soft(current, gradient, cutoff, active):
@@ -46,7 +56,7 @@
         gathered = lax.all_to_all(partial, "snp", 0, 0, tiled=False)
         prediction = jnp.sum(gathered.astype(jnp.float32), axis=0)
         residual = (responses - prediction).astype(jnp.bfloat16)
-        shard_rows = lax.all_gather(residual, "snp", axis=0, tiled=True)
+        shard_rows = gather_by_hops(residual, "snp", 0)
         blocks = shard_rows.reshape(slot_total, tile_width, sample_count)
         full = jnp.einsum(
             "jps,sbk->jbpk", blocks, geno_blocks, preferred_element_type=jnp.float32

time: 483 us -> 525 us (1.087)
  waiting for transfers between devices: 287 us -> 320 us
  other arithmetic: 20.2 us -> 29.8 us
    ppermute x0 -> x14, waiting for transfers between devices: none -> 139 us  [gather_by_hops(): lax.ppermute(current, axis, [(i, (i + 1) % n_dev) for i in range(n_dev)])]
    all_gather x2 -> x0, waiting for transfers between devices: 102 us -> none  [per_device(): shard_rows = lax.all_gather(residual, 'snp', axis=0, tiled=True)]
    concatenate x0 -> x2, other arithmetic: none -> 10.9 us  [gather_by_hops(): jnp.roll(row_of_blocks, (lax.axis_index(axis) + 1) * x.shape[dim], axis=dim)]
  transfers between devices with their start and end apart: 8 -> 20, of which waited for: 8 -> 20; matrix products, arithmetic and copies ran while one was open for 0% -> 0% of each run, Pallas kernels for 0% -> 0%
where the time goes in v1:
time: 525 us
  waiting for transfers between devices  320 us (61%)
  blocking collectives  121 us (23%)
  other arithmetic  29.8 us (6%)
  matrix products  18.4 us (4%)
  local copies, waits for them, and re-layouts  17.6 us (3%)
  between operations  14.4 us (3%)
    ppermute x14, waiting for transfers between devices, gather_by_hops(): lax.ppermute(current, axis, [(i, (i + 1) % n_dev) for i in range(n_dev)])  139 us
    psum x2, waiting for transfers between devices, per_device(): part = lax.psum(part, 'sx')  133 us
    all_to_all x2, blocking collectives, per_device(): gathered = lax.all_to_all(partial, 'snp', 0, 0, tiled=False)  121 us
    all_gather x2, waiting for transfers between devices, per_device(): gradient = lax.all_gather(part, 'sc', axis=0, tiled=True)  29.9 us
    reduce_scatter x2, waiting for transfers between devices, per_device(): lax.psum_scatter(local_gradient, 'sc', scatter_dimension=0, tiled=True)  18.8 us
    gather x2, local copies, waits for them, and re-layouts, per_device(): local_gradient = jnp.take(full, cell, axis=0, mode='clip')  12.1 us
    concatenate x2, other arithmetic, gather_by_hops(): jnp.roll(row_of_blocks, (lax.axis_index(axis) + 1) * x.shape[dim], axis=dim)  10.9 us
  transfers between devices with their start and end apart: 20, of which 20 were waited for; matrix products, arithmetic and copies ran while one was open for 0% of the time, Pallas kernels for 0%

profile of v1, /device:TPU:0, one launch (start us, length us, event | category | flops | bytes accessed | tf_op | source)
XLA Modules:
  0.0 524.7 jit_solution(5346652362206630392)
XLA Ops:
  7.2 0.7 slice_bitcast_fusion
  7.9 0.7 select_reduce_fusion.1
  8.6 0.7 fusion.9
  9.3 1.3 copy.36
  10.6 2.6 select_convert_fusion
  13.2 2.0 convolution_convert_fusion.1
  15.3 1.0 copy.35
  16.3 2.6 bitcast_convert_fusion.1
  18.9 60.9 %all_to_all.10 = bf16[8,384,384]{2,1,0:T(8,128)(2,1)S(1)} all-to-all(bf16[8,384,384]{2,1,0:T(8,128)(2,1)S(1)} %bitcast.64), channel_id=1, replica_groups=mesh['snp'=8,'sx'=2,'sc'=2] {'snp'}, dimensions={0} | all-to-all | bytes 4718592 | tf_op jit(solution)/shard_map/all_to_all | solution.py:56
  79.9 0.3 convert_reduce_fusion.1
  80.2 0.7 copy-done
  80.9 0.1 subtract_convert_fusion.1
  81.0 1.5 collective-permute-start
  82.5 8.9 %collective-permute-done = bf16[384,384]{1,0:T(8,128)(2,1)S(1)} collective-permute-done((bf16[384,384]{1,0:T(8,128)(2,1)S(1)}, bf16[384,384]{1,0:T(8,128)(2,1)S(1)}, u32[]{:S(2)}, u32[]{:S(2)}) %collective-permute-start) | collective-permute-done | bytes 294944 | tf_op jit(solution)/shard_map/ppermute | solution.py:14
  91.4 0.0 collective-permute-start.1
  91.4 9.4 %collective-permute-done.1 = bf16[384,384]{1,0:T(8,128)(2,1)S(1)} collective-permute-done((bf16[384,384]{1,0:T(8,128)(2,1)S(1)}, bf16[384,384]{1,0:T(8,128)(2,1)S(1)}, u32[]{:S(2)}, u32[]{:S(2)}) %collective-permute-start.1) | collective-permute-done | bytes 294944 | tf_op jit(solution)/shard_map/ppermute | solution.py:14
  100.8 9.4 %collective-permute-done.2 = bf16[384,384]{1,0:T(8,128)(2,1)S(1)} collective-permute-done((bf16[384,384]{1,0:T(8,128)(2,1)S(1)}, bf16[384,384]{1,0:T(8,128)(2,1)S(1)}, u32[]{:S(2)}, u32[]{:S(2)}) %collective-permute-start.2) | collective-permute-done | bytes 294944 | tf_op jit(solution)/shard_map/ppermute | solution.py:14
  110.2 9.7 %collective-permute-done.3 = bf16[384,384]{1,0:T(8,128)(2,1)S(1)} collective-permute-done((bf16[384,384]{1,0:T(8,128)(2,1)S(1)}, bf16[384,384]{1,0:T(8,128)(2,1)S(1)}, u32[]{:S(2)}, u32[]{:S(2)}) %collective-permute-start.3) | collective-permute-done | bytes 294944 | tf_op jit(solution)/shard_map/ppermute | solution.py:14
  120.0 10.8 %collective-permute-done.4 = bf16[384,384]{1,0:T(8,128)(2,1)S(1)} collective-permute-done((bf16[384,384]{1,0:T(8,128)(2,1)S(1)}, bf16[384,384]{1,0:T(8,128)(2,1)S(1)}, u32[]{:S(2)}, u32[]{:S(2)}) %collective-permute-start.4) | collective-permute-done | bytes 294944 | tf_op jit(solution)/shard_map/ppermute | solution.py:14
  130.8 12.0 %collective-permute-done.5 = bf16[384,384]{1,0:T(8,128)(2,1)S(1)} collective-permute-done((bf16[384,384]{1,0:T(8,128)(2,1)S(1)}, bf16[384,384]{1,0:T(8,128)(2,1)S(1)}, u32[]{:S(2)}, u32[]{:S(2)}) %collective-permute-start.5) | collective-permute-done | bytes 294944 | tf_op jit(solution)/shard_map/ppermute | solution.py:14
  142.8 0.0 collective-permute-start.6
  142.8 9.4 %collective-permute-done.6 = bf16[384,384]{1,0:T(8,128)(2,1)S(1)} collective-permute-done((bf16[384,384]{1,0:T(8,128)(2,1)S(1)}, bf16[384,384]{1,0:T(8,128)(2,1)S(1)}, u32[]{:S(2)}, u32[]{:S(2)}) %collective-permute-start.6) | collective-permute-done | bytes 294944 | tf_op jit(solution)/shard_map/ppermute | solution.py:14
  152.6 5.5 %fusion.1 = bf16[3072,384]{1,0:T(8,128)(2,1)S(1)} fusion(s32[]{:T(128)S(6)} %select_n.36, bf16[3072,384]{1,0:T(8,128)(2,1)S(1)} %constant_dynamic-update-slice_fusion), kind=kLoop, calls=%fused_computation.16 | loop fusion | flops 4718592 | bytes 4718596 | tf_op jit(solution)/shard_map/jit(_roll_dynamic)/concatenate | solution.py:17
  158.1 4.6 fusion.11
  162.7 6.1 %gather_fusion = f32[128,64,128]{2,1,0:T(8,128)} fusion(f32[240,64,128]{2,1,0:T(8,128)} %bitcast.55, s32[1024]{0:T(1024)S(1)} %pad_clamp_fusion), kind=kCustom, calls=%fused_computation | custom fusion | bytes 8389120 | tf_op jit(solution)/shard_map/jit(_take)/gather | solution.py:64
  168.7 0.0 reduce-scatter.3.cloned.1.call-update
  168.7 0.0 copy-start.1
  168.8 0.0 all-reduce.3.cloned.1.call-start
  168.8 9.4 %reduce-scatter.3.cloned.1.call-done = f32[64,64,128]{2,1,0:T(8,128)} async-done(((f32[128,64,128]{2,1,0:T(8,128)}), f32[64,64,128]{2,1,0:T(8,128)}) %reduce-scatter.3.cloned.1.call-update) | async-done | bytes 2097168 | tf_op jit(solution)/shard_map/reduce_scatter | solution.py:66
  178.2 0.0 all-reduce.3.cloned.1.call-update
  178.2 0.0 all-gather.3.cloned.1.call-start
  178.3 66.6 %all-reduce.3.cloned.1.call-done = f32[64,64,128]{2,1,0:T(8,128)} async-done(((f32[64,64,128]{2,1,0:T(8,128)}), f32[64,64,128]{2,1,0:T(8,128)}) %all-reduce.3.cloned.1.call-update) | async-done | bytes 2097168 | tf_op jit(solution)/shard_map/psum | solution.py:67
  244.8 0.0 all-gather.3.cloned.1.call-update
  244.9 0.3 reduce-scatter.5.cloned.1.call-start
  245.1 0.1 select_reduce_fusion
  245.2 14.9 %all-gather.3.cloned.1.call-done = f32[128,64,128]{2,1,0:T(8,128)} async-done(((f32[64,64,128]{2,1,0:T(8,128)}), f32[128,64,128]{2,1,0:T(8,128)}) %all-gather.3.cloned.1.call-update) | async-done | bytes 4194320 | tf_op jit(solution)/shard_map/all_gather | solution.py:68
  260.1 4.7 fusion.10
  264.8 2.0 convolution_convert_fusion
  266.9 1.0 copy.40
  267.9 2.6 bitcast_convert_fusion
  270.5 59.8 %all_to_all.11 = bf16[8,384,384]{2,1,0:T(8,128)(2,1)S(1)} all-to-all(bf16[8,384,384]{2,1,0:T(8,128)(2,1)S(1)} %bitcast.65), channel_id=1, replica_groups=mesh['snp'=8,'sx'=2,'sc'=2] {'snp'}, dimensions={0} | all-to-all | bytes 4718592 | tf_op jit(solution)/shard_map/all_to_all | solution.py:56
  330.4 0.3 convert_reduce_fusion
  330.7 0.1 subtract_convert_fusion
  330.8 1.5 collective-permute-start.7
  332.3 9.3 %collective-permute-done.7 = bf16[384,384]{1,0:T(8,128)(2,1)S(1)} collective-permute-done((bf16[384,384]{1,0:T(8,128)(2,1)S(1)}, bf16[384,384]{1,0:T(8,128)(2,1)S(1)}, u32[]{:S(2)}, u32[]{:S(2)}) %collective-permute-start.7) | collective-permute-done | bytes 294944 | tf_op jit(solution)/shard_map/ppermute | solution.py:14
  341.6 9.9 %collective-permute-done.8 = bf16[384,384]{1,0:T(8,128)(2,1)S(1)} collective-permute-done((bf16[384,384]{1,0:T(8,128)(2,1)S(1)}, bf16[384,384]{1,0:T(8,128)(2,1)S(1)}, u32[]{:S(2)}, u32[]{:S(2)}) %collective-permute-start.8) | collective-permute-done | bytes 294944 | tf_op jit(solution)/shard_map/ppermute | solution.py:14
  351.5 9.4 %collective-permute-done.9 = bf16[384,384]{1,0:T(8,128)(2,1)S(1)} collective-permute-done((bf16[384,384]{1,0:T(8,128)(2,1)S(1)}, bf16[384,384]{1,0:T(8,128)(2,1)S(1)}, u32[]{:S(2)}, u32[]{:S(2)}) %collective-permute-start.9) | collective-permute-done | bytes 294944 | tf_op jit(solution)/shard_map/ppermute | solution.py:14
  360.9 9.4 %collective-permute-done.10 = bf16[384,384]{1,0:T(8,128)(2,1)S(1)} collective-permute-done((bf16[384,384]{1,0:T(8,128)(2,1)S(1)}, bf16[384,384]{1,0:T(8,128)(2,1)S(1)}, u32[]{:S(2)}, u32[]{:S(2)}) %collective-permute-start.10) | collective-permute-done | bytes 294944 | tf_op jit(solution)/shard_map/ppermute | solution.py:14
  370.3 10.2 %collective-permute-done.11 = bf16[384,384]{1,0:T(8,128)(2,1)S(1)} collective-permute-done((bf16[384,384]{1,0:T(8,128)(2,1)S(1)}, bf16[384,384]{1,0:T(8,128)(2,1)S(1)}, u32[]{:S(2)}, u32[]{:S(2)}) %collective-permute-start.11) | collective-permute-done | bytes 294944 | tf_op jit(solution)/shard_map/ppermute | solution.py:14
  380.5 11.3 %collective-permute-done.12 = bf16[384,384]{1,0:T(8,128)(2,1)S(1)} collective-permute-done((bf16[384,384]{1,0:T(8,128)(2,1)S(1)}, bf16[384,384]{1,0:T(8,128)(2,1)S(1)}, u32[]{:S(2)}, u32[]{:S(2)}) %collective-permute-start.12) | collective-permute-done | bytes 294944 | tf_op jit(solution)/shard_map/ppermute | solution.py:14
  391.8 0.0 collective-permute-start.13
  391.8 9.4 %collective-permute-done.13 = bf16[384,384]{1,0:T(8,128)(2,1)S(1)} collective-permute-done((bf16[384,384]{1,0:T(8,128)(2,1)S(1)}, bf16[384,384]{1,0:T(8,128)(2,1)S(1)}, u32[]{:S(2)}, u32[]{:S(2)}) %collective-permute-start.13) | collective-permute-done | bytes 294944 | tf_op jit(solution)/shard_map/ppermute | solution.py:14
  401.7 5.5 %fusion = bf16[3072,384]{1,0:T(8,128)(2,1)S(1)} fusion(s32[]{:T(128)S(6)} %select_n.36, bf16[3072,384]{1,0:T(8,128)(2,1)S(1)} %constant_dynamic-update-slice_fusion.8), kind=kLoop, calls=%fused_computation.15 | loop fusion | flops 4718592 | bytes 4718596 | tf_op jit(solution)/shard_map/jit(_roll_dynamic)/concatenate | solution.py:17
  407.1 4.5 fusion.12
  411.7 6.1 %gather_fusion.1 = f32[128,64,128]{2,1,0:T(8,128)} fusion(f32[240,64,128]{2,1,0:T(8,128)} %bitcast.54, s32[1024]{0:T(1024)S(1)} %pad_clamp_fusion), kind=kCustom, calls=%fused_computation.1 | custom fusion | bytes 8389120 | tf_op jit(solution)/shard_map/jit(_take)/gather | solution.py:64
  417.8 0.0 reduce-scatter.5.cloned.1.call-update
  417.8 0.0 all-reduce.5.cloned.1.call-start
  417.8 9.4 %reduce-scatter.5.cloned.1.call-done = f32[64,64,128]{2,1,0:T(8,128)} async-done(((f32[128,64,128]{2,1,0:T(8,128)}), f32[64,64,128]{2,1,0:T(8,128)}) %reduce-scatter.5.cloned.1.call-update) | async-done | bytes 2097168 | tf_op jit(solution)/shard_map/reduce_scatter | solution.py:66
  427.2 0.0 all-reduce.5.cloned.1.call-update
  427.3 0.0 all-gather.5.cloned.1.call-start
  427.3 66.4 %all-reduce.5.cloned.1.call-done = f32[64,64,128]{2,1,0:T(8,128)} async-done(((f32[64,64,128]{2,1,0:T(8,128)}), f32[64,64,128]{2,1,0:T(8,128)}) %all-reduce.5.cloned.1.call-update) | async-done | bytes 2097168 | tf_op jit(solution)/shard_map/psum | solution.py:67
  493.7 0.0 all-gather.5.cloned.1.call-update
  493.7 15.1 %all-gather.5.cloned.1.call-done = f32[128,64,128]{2,1,0:T(8,128)} async-done(((f32[64,64,128]{2,1,0:T(8,128)}), f32[128,64,128]{2,1,0:T(8,128)}) %all-gather.5.cloned.1.call-update) | async-done | bytes 4194320 | tf_op jit(solution)/shard_map/all_gather | solution.py:68
  508.8 9.1 %multiply_select_fusion = f32[128,64,128]{2,1,0:T(8,128)} fusion(f32[128,64,128]{2,1,0:T(8,128)} %all-gather.5.cloned.1.call-done, f32[128]{0:T(128)S(1)} %broadcast_multiply_fusion, pred[128]{0:T(512)(128)(4,1)S(1)} %iota_compare_fusion.2, f32[128,64,128]{2,1,0:T(8,128)} %all-gather.3.cloned.1.call-done, f32[128,64,128]{2,1,0:T(8,128)} %param.11), kind=kLoop, calls=%fused_computation.10 | loop fusion | flops 17825792 | bytes 16777856 | tf_op jit(solution)/shard_map/jit(_where)/select_n | solution.py:23
  (31 shorter events, 0.8 us)
Async XLA Ops:
  6.5 171.7 %reduce-scatter.3.cloned.1.call-start = ((), (), s32[]{:S(2)}) async-start(), calls=%async_computation.4 | async-start | bytes 6291456 | tf_op jit(solution)/shard_map/reduce_scatter | solution.py:66
  79.9 1.1 copy-start
  81.0 10.4 %collective-permute-start = (bf16[384,384]{1,0:T(8,128)(2,1)S(1)}, bf16[384,384]{1,0:T(8,128)(2,1)S(1)}, u32[]{:S(2)}, u32[]{:S(2)}) collective-permute-start(bf16[384,384]{1,0:T(8,128)(2,1)S(1)} %subtract_convert_fusion.1), channel_id=1, source_target_pairs={{0,4},{4,8},{8,12},{12,16},{16,20},{20,24},{24,28},{28,0},{1,5},{5... | collective-permute-start | bytes 884744 | tf_op jit(solution)/shard_map/ppermute | solution.py:14
  91.4 9.4 %collective-permute-start.1 = (bf16[384,384]{1,0:T(8,128)(2,1)S(1)}, bf16[384,384]{1,0:T(8,128)(2,1)S(1)}, u32[]{:S(2)}, u32[]{:S(2)}) collective-permute-start(bf16[384,384]{1,0:T(8,128)(2,1)S(1)} %collective-permute-done), channel_id=1, source_target_pairs={{0,4},{4,8},{8,12},{12,16},{16,20},{20,24},{24,28},{28,0},{1,5},{5... | collective-permute-start | bytes 884744 | tf_op jit(solution)/shard_map/ppermute | solution.py:14
  100.8 9.4 %collective-permute-start.2 = (bf16[384,384]{1,0:T(8,128)(2,1)S(1)}, bf16[384,384]{1,0:T(8,128)(2,1)S(1)}, u32[]{:S(2)}, u32[]{:S(2)}) collective-permute-start(bf16[384,384]{1,0:T(8,128)(2,1)S(1)} %collective-permute-done.1), channel_id=1, source_target_pairs={{0,4},{4,8},{8,12},{12,16},{16,20},{20,24},{24,28},{28,0},{1,5},{5... | collective-permute-start | bytes 884744 | tf_op jit(solution)/shard_map/ppermute | solution.py:14
  110.2 9.7 %collective-permute-start.3 = (bf16[384,384]{1,0:T(8,128)(2,1)S(1)}, bf16[384,384]{1,0:T(8,128)(2,1)S(1)}, u32[]{:S(2)}, u32[]{:S(2)}) collective-permute-start(bf16[384,384]{1,0:T(8,128)(2,1)S(1)} %collective-permute-done.2), channel_id=1, source_target_pairs={{0,4},{4,8},{8,12},{12,16},{16,20},{20,24},{24,28},{28,0},{1,5},{5... | collective-permute-start | bytes 884744 | tf_op jit(solution)/shard_map/ppermute | solution.py:14
  120.0 10.8 %collective-permute-start.4 = (bf16[384,384]{1,0:T(8,128)(2,1)S(1)}, bf16[384,384]{1,0:T(8,128)(2,1)S(1)}, u32[]{:S(2)}, u32[]{:S(2)}) collective-permute-start(bf16[384,384]{1,0:T(8,128)(2,1)S(1)} %collective-permute-done.3), channel_id=1, source_target_pairs={{0,4},{4,8},{8,12},{12,16},{16,20},{20,24},{24,28},{28,0},{1,5},{5... | collective-permute-start | bytes 884744 | tf_op jit(solution)/shard_map/ppermute | solution.py:14
  130.8 12.0 %collective-permute-start.5 = (bf16[384,384]{1,0:T(8,128)(2,1)S(1)}, bf16[384,384]{1,0:T(8,128)(2,1)S(1)}, u32[]{:S(2)}, u32[]{:S(2)}) collective-permute-start(bf16[384,384]{1,0:T(8,128)(2,1)S(1)} %collective-permute-done.4), channel_id=1, source_target_pairs={{0,4},{4,8},{8,12},{12,16},{16,20},{20,24},{24,28},{28,0},{1,5},{5... | collective-permute-start | bytes 884744 | tf_op jit(solution)/shard_map/ppermute | solution.py:14
  142.8 9.4 %collective-permute-start.6 = (bf16[384,384]{1,0:T(8,128)(2,1)S(1)}, bf16[384,384]{1,0:T(8,128)(2,1)S(1)}, u32[]{:S(2)}, u32[]{:S(2)}) collective-permute-start(bf16[384,384]{1,0:T(8,128)(2,1)S(1)} %collective-permute-done.5), channel_id=1, source_target_pairs={{0,4},{4,8},{8,12},{12,16},{16,20},{20,24},{24,28},{28,0},{1,5},{5... | collective-permute-start | bytes 884744 | tf_op jit(solution)/shard_map/ppermute | solution.py:14
  168.7 76.4 %copy-start.1 = (f32[46]{0:T(128)S(1)}, f32[46]{0:T(128)}, u32[]{:S(2)}) copy-start(f32[46]{0:T(128)} %param.15) | copy-start | bytes 556
  168.8 76.1 %all-reduce.3.cloned.1.call-start = ((), (), s32[]{:S(2)}) async-start(), calls=%async_computation.5 | async-start | bytes 4194304 | tf_op jit(solution)/shard_map/psum | solution.py:67
  178.2 81.9 %all-gather.3.cloned.1.call-start = ((), (), s32[]{:S(2)}) async-start(), calls=%async_computation.6 | async-start | bytes 6291456 | tf_op jit(solution)/shard_map/all_gather | solution.py:68
  244.9 182.4 %reduce-scatter.5.cloned.1.call-start = ((), (), s32[]{:S(2)}) async-start(), calls=%async_computation.7 | async-start | bytes 6291456 | tf_op jit(solution)/shard_map/reduce_scatter | solution.py:66
  330.8 10.8 %collective-permute-start.7 = (bf16[384,384]{1,0:T(8,128)(2,1)S(1)}, bf16[384,384]{1,0:T(8,128)(2,1)S(1)}, u32[]{:S(2)}, u32[]{:S(2)}) collective-permute-start(bf16[384,384]{1,0:T(8,128)(2,1)S(1)} %subtract_convert_fusion), channel_id=1, source_target_pairs={{0,4},{4,8},{8,12},{12,16},{16,20},{20,24},{24,28},{28,0},{1,5},{5... | collective-permute-start | bytes 884744 | tf_op jit(solution)/shard_map/ppermute | solution.py:14
  341.6 9.9 %collective-permute-start.8 = (bf16[384,384]{1,0:T(8,128)(2,1)S(1)}, bf16[384,384]{1,0:T(8,128)(2,1)S(1)}, u32[]{:S(2)}, u32[]{:S(2)}) collective-permute-start(bf16[384,384]{1,0:T(8,128)(2,1)S(1)} %collective-permute-done.7), channel_id=1, source_target_pairs={{0,4},{4,8},{8,12},{12,16},{16,20},{20,24},{24,28},{28,0},{1,5},{5... | collective-permute-start | bytes 884744 | tf_op jit(solution)/shard_map/ppermute | solution.py:14
  351.5 9.4 %collective-permute-start.9 = (bf16[384,384]{1,0:T(8,128)(2,1)S(1)}, bf16[384,384]{1,0:T(8,128)(2,1)S(1)}, u32[]{:S(2)}, u32[]{:S(2)}) collective-permute-start(bf16[384,384]{1,0:T(8,128)(2,1)S(1)} %collective-permute-done.8), channel_id=1, source_target_pairs={{0,4},{4,8},{8,12},{12,16},{16,20},{20,24},{24,28},{28,0},{1,5},{5... | collective-permute-start | bytes 884744 | tf_op jit(solution)/shard_map/ppermute | solution.py:14
  360.9 9.4 %collective-permute-start.10 = (bf16[384,384]{1,0:T(8,128)(2,1)S(1)}, bf16[384,384]{1,0:T(8,128)(2,1)S(1)}, u32[]{:S(2)}, u32[]{:S(2)}) collective-permute-start(bf16[384,384]{1,0:T(8,128)(2,1)S(1)} %collective-permute-done.9), channel_id=1, source_target_pairs={{0,4},{4,8},{8,12},{12,16},{16,20},{20,24},{24,28},{28,0},{1,5},{5... | collective-permute-start | bytes 884744 | tf_op jit(solution)/shard_map/ppermute | solution.py:14
  370.3 10.2 %collective-permute-start.11 = (bf16[384,384]{1,0:T(8,128)(2,1)S(1)}, bf16[384,384]{1,0:T(8,128)(2,1)S(1)}, u32[]{:S(2)}, u32[]{:S(2)}) collective-permute-start(bf16[384,384]{1,0:T(8,128)(2,1)S(1)} %collective-permute-done.10), channel_id=1, source_target_pairs={{0,4},{4,8},{8,12},{12,16},{16,20},{20,24},{24,28},{28,0},{1,5},{5... | collective-permute-start | bytes 884744 | tf_op jit(solution)/shard_map/ppermute | solution.py:14
  380.5 11.3 %collective-permute-start.12 = (bf16[384,384]{1,0:T(8,128)(2,1)S(1)}, bf16[384,384]{1,0:T(8,128)(2,1)S(1)}, u32[]{:S(2)}, u32[]{:S(2)}) collective-permute-start(bf16[384,384]{1,0:T(8,128)(2,1)S(1)} %collective-permute-done.11), channel_id=1, source_target_pairs={{0,4},{4,8},{8,12},{12,16},{16,20},{20,24},{24,28},{28,0},{1,5},{5... | collective-permute-start | bytes 884744 | tf_op jit(solution)/shard_map/ppermute | solution.py:14
  391.8 9.4 %collective-permute-start.13 = (bf16[384,384]{1,0:T(8,128)(2,1)S(1)}, bf16[384,384]{1,0:T(8,128)(2,1)S(1)}, u32[]{:S(2)}, u32[]{:S(2)}) collective-permute-start(bf16[384,384]{1,0:T(8,128)(2,1)S(1)} %collective-permute-done.12), channel_id=1, source_target_pairs={{0,4},{4,8},{8,12},{12,16},{16,20},{20,24},{24,28},{28,0},{1,5},{5... | collective-permute-start | bytes 884744 | tf_op jit(solution)/shard_map/ppermute | solution.py:14
  417.8 75.9 %all-reduce.5.cloned.1.call-start = ((), (), s32[]{:S(2)}) async-start(), calls=%async_computation.8 | async-start | bytes 4194304 | tf_op jit(solution)/shard_map/psum | solution.py:67
  427.3 81.5 %all-gather.5.cloned.1.call-start = ((), (), s32[]{:S(2)}) async-start(), calls=%async_computation.9 | async-start | bytes 6291456 | tf_op jit(solution)/shard_map/all_gather | solution.py:68
Sparse Core Ops, SparseCore 0:
  168.9 9.2 reduce-scatter.2
  180.6 64.2 all-reduce.2
  246.4 13.6 all-gather.2
  417.9 9.2 reduce-scatter.4
  429.5 64.1 all-reduce.4
  495.1 13.6 all-gather.4
